TPU v7x, 512 devices: a whole 4x4x16 slice. The times are simulated.
512 devices in a mesh: dp: 64 (over z, x_lo, core), tensor: 8 (over y, x_hi).
Axes of the slice: x: 4 (x_hi: 2, x_lo: 2; x = x_hi * 2 + x_lo), y: 4, z: 16, core: 2. Of those that a mesh axis runs over, the one named last changes fastest.
Arguments:
- hidden_in: bfloat16 [16384, 4096], P(('dp', 'tensor')), may hold values from -12 to 12
- norm_gain: bfloat16 [4096], replicated, may hold values from 0.5 to 1.5
- w_query: bfloat16 [4096, 4096], P('dp', 'tensor'), may hold values from -0.11328125 to 0.11328125
- w_key: bfloat16 [4096, 1024], P('dp', 'tensor'), may hold values from -0.11328125 to 0.11328125
- w_value: bfloat16 [4096, 1024], P('dp', 'tensor'), may hold values from -0.09375 to 0.09375
- w_out: bfloat16 [4096, 4096], P('tensor', 'dp'), may hold values from -0.09375 to 0.09375
- segment: int32 [16384], P('dp'), may hold values from -1 to 1, as said below
Outputs:
- hidden_out: bfloat16 [16384, 4096], P(('dp', 'tensor'))
- kv_cache: bfloat16 [16384, 8, 256], P('dp', 'tensor')
Inputs may be any that keep to these rules, and one draw needn't show every extreme that they name: `segment`: within each pack of 256 rows, prompts are numbered from 0 in order and each starts at a multiple of 128; a prompt's last tile may end in rows of -1, and whole tiles of -1 may only follow the last prompt of a pack; the first tile of every pack holds a prompt; in every draw some pack has no tile of -1 only and holds one prompt a tile.
All inputs are finite; a program needn't handle non-finite values.
Results may differ from a plain program's by a relative error of at most 0.0085.
Values may be sent and summed in bfloat16 or wider, within the bound.
No kernel may reach another device: no remote copies, remote signals or barrier semaphores. Data moves between devices by JAX's collectives and lax.ppermute only.
A program may use at most 64 MiB of HBM per device.

v0:
```python
import jax
import jax.numpy as jnp
from jax import lax
from jax.sharding import PartitionSpec as P

HEAD = 128
rope_theta = 500000.0
norm_epsilon = 1e-05


def inverse_frequency(head_width):
    exponent = jnp.arange(0, head_width, 2).astype(jnp.float32) / head_width
    base_freq = rope_theta ** (-exponent)
    wavelength = 2.0 * jnp.pi / base_freq
    smooth = (8192.0 / wavelength - 1.0) / 3.0
    blended = (1.0 - smooth) * base_freq / 8.0 + smooth * base_freq
    return jnp.where(
        wavelength < 2048.0, base_freq, jnp.where(wavelength > 8192.0, base_freq / 8.0, blended)
    )


def positions_of(segment):
    row_index = jnp.arange(segment.shape[0], dtype=jnp.int32)
    changed = jnp.concatenate([jnp.ones((1,), dtype=bool), segment[1:] != segment[:-1]])
    begins = lax.cummax(jnp.where(changed, row_index, 0), axis=0)
    return row_index - begins


def rotate(vectors, position):
    head_width = vectors.shape[-1]
    half_width = head_width // 2
    angles = position.astype(jnp.float32)[:, None] * inverse_frequency(head_width)[None, :]
    cosine = jnp.concatenate([jnp.cos(angles), jnp.cos(angles)], axis=-1)[:, None, :]
    sine_table = jnp.concatenate([jnp.sin(angles), jnp.sin(angles)], axis=-1)[:, None, :]
    turned = jnp.concatenate([-vectors[..., half_width:], vectors[..., :half_width]], axis=-1)
    return vectors * cosine + turned * sine_table


def rms_normed(rows_float, norm_gain):
    mean_square = jnp.mean(rows_float * rows_float, axis=-1, keepdims=True)
    return (
        rows_float * lax.rsqrt(mean_square + norm_epsilon) * norm_gain.astype(jnp.float32)
    ).astype(jnp.bfloat16)


def visible_pairs(segment, key_count):
    row_index = jnp.arange(segment.shape[0], dtype=jnp.int32)
    key_index = jnp.arange(key_count, dtype=jnp.int32)
    same_segment = (segment[:, None] == segment[None, :]) & (segment[:, None] >= 0)
    causal = key_index[None, :] <= row_index[:, None]
    return same_segment & causal | (key_index[None, :] == row_index[:, None])


def body(hidden_in, norm_gain, w_query, w_key, w_value, w_out, segment):
    pack_rows = segment.shape[0]
    query_cols = w_query.shape[1]
    kv_cols = w_key.shape[1]
    query_heads = query_cols // HEAD
    kv_heads = kv_cols // HEAD
    group_size = query_heads // kv_heads
    score_scale = HEAD ** (-0.5)
    rows_float = hidden_in.astype(jnp.float32)
    normed = rms_normed(rows_float, norm_gain)
    gathered = lax.all_gather(normed, "tensor", axis=0, tiled=True)
    joined = jnp.concatenate(
        (
            lax.all_gather(w_query, "dp", axis=0, tiled=True),
            lax.all_gather(w_key, "dp", axis=0, tiled=True),
            lax.all_gather(w_value, "dp", axis=0, tiled=True),
        ),
        axis=1,
    )
    projected = jnp.dot(gathered, joined, preferred_element_type=jnp.float32)
    position = positions_of(segment)
    query_rows = rotate(
        projected[:, :query_cols].reshape(pack_rows, query_heads, HEAD), position
    ).astype(jnp.bfloat16)
    key_rows = rotate(
        projected[:, query_cols : query_cols + kv_cols].reshape(pack_rows, kv_heads, HEAD), position
    ).astype(jnp.bfloat16)
    value_rows = (
        projected[:, query_cols + kv_cols :].astype(jnp.bfloat16).reshape(pack_rows, kv_heads, HEAD)
    )
    cache_rows = jnp.concatenate([key_rows, value_rows], axis=-1)
    grouped_query = query_rows.reshape(pack_rows, kv_heads, group_size, HEAD)
    scores = (
        jnp.einsum("skgh,tkh->kgst", grouped_query, key_rows, preferred_element_type=jnp.float32)
        * score_scale
    )
    allowed = visible_pairs(segment, pack_rows)
    scores = jnp.where(allowed, scores, -1e30)
    row_max = jnp.max(scores, axis=-1, keepdims=True)
    weight = jnp.exp(scores - row_max)
    weight_sum = jnp.sum(weight, axis=-1)
    mixed_rows = (
        jnp.einsum(
            "kgst,tkh->kgsh",
            weight.astype(jnp.bfloat16),
            value_rows,
            preferred_element_type=jnp.float32,
        )
        / weight_sum[..., None]
    )
    attended = (
        jnp.transpose(mixed_rows, (2, 0, 1, 3)).astype(jnp.bfloat16).reshape(pack_rows, query_cols)
    )
    out_full = lax.all_gather(w_out, "dp", axis=1, tiled=True)
    summed = lax.psum_scatter(
        jnp.dot(attended, out_full, preferred_element_type=jnp.float32).astype(jnp.bfloat16),
        "tensor",
        scatter_dimension=0,
        tiled=True,
    ).astype(jnp.float32)
    hidden_out = (summed + rows_float).astype(jnp.bfloat16)
    return (hidden_out, cache_rows)


def solution(mesh):
    return jax.shard_map(
        body,
        mesh=mesh,
        in_specs=(
            P(("dp", "tensor"), None),
            P(),
            P("dp", "tensor"),
            P("dp", "tensor"),
            P("dp", "tensor"),
            P("tensor", "dp"),
            P("dp"),
        ),
        out_specs=(P(("dp", "tensor"), None), P("dp", "tensor", None)),
        check_vma=False,
    )
```

profile of v0, /device:TPU:32, one launch (start us, length us, event | category | flops | bytes accessed | tf_op | source)
XLA Modules:
  0.0 671.7 jit_solution(11263055543441471757)
XLA Ops:
  7.2 0.0 all-gather.10.cloned.1.call-start
  7.2 0.7 all-gather.10.cloned.1.call-update
  7.9 0.0 all-gather.12.cloned.1.call-start
  7.9 0.7 all-gather.12.cloned.1.call-update
  8.6 0.0 all-gather.6.cloned.1.call-start
  8.7 0.7 convert_element_type.62
  9.4 1.1 fusion.11
  10.5 1.8 fusion.13
  12.3 0.0 all-gather.6.cloned.1.call-update
  12.3 0.0 all-gather.8.cloned.1.call-start
  12.4 0.5 all-gather.8.cloned.1.call-update
  12.9 0.0 all-gather.14.cloned.1.call-start
  13.0 0.5 all-gather.14.cloned.1.call-update
  13.5 0.0 reduce-scatter.2.cloned.1.call-start
  13.5 0.8 slice_compare_fusion
  14.4 0.1 fusion.30
  14.5 0.3 reduce-window.9
  14.8 0.1 slice.38
  14.9 0.1 slice_reduce_fusion
  15.0 0.7 broadcast_compare_fusion
  15.7 0.1 fusion.31
  15.8 0.9 fusion.23
  16.6 0.5 multiply_cosine_fusion
  17.2 118.4 %all-gather.10.cloned.1.call-done = bf16[4096,128]{1,0:T(8,128)(2,1)} async-done(((bf16[64,128]{1,0:T(8,128)(2,1)}), bf16[4096,128]{1,0:T(8,128)(2,1)}) %all-gather.10.cloned.1.call-update) | async-done | bytes 1048592 | tf_op jit(solution)/shard_map/all_gather | solution.py:68
  135.6 119.9 %all-gather.12.cloned.1.call-done = bf16[4096,128]{1,0:T(8,128)(2,1)} async-done(((bf16[64,128]{1,0:T(8,128)(2,1)}), bf16[4096,128]{1,0:T(8,128)(2,1)}) %all-gather.12.cloned.1.call-update) | async-done | bytes 1048592 | tf_op jit(solution)/shard_map/all_gather | solution.py:69
  255.5 69.0 %all-gather.6.cloned.1.call-done = bf16[256,4096]{1,0:T(8,128)(2,1)} async-done(((bf16[32,4096]{1,0:T(8,128)(2,1)}), bf16[256,4096]{1,0:T(8,128)(2,1)}) %all-gather.6.cloned.1.call-update) | async-done | bytes 2097168 | tf_op jit(solution)/shard_map/all_gather | solution.py:64
  324.5 123.7 %all-gather.8.cloned.1.call-done = bf16[4096,512]{1,0:T(8,128)(2,1)} async-done(((bf16[64,512]{1,0:T(8,128)(2,1)}), bf16[4096,512]{1,0:T(8,128)(2,1)}) %all-gather.8.cloned.1.call-update) | async-done | bytes 4194320 | tf_op jit(solution)/shard_map/all_gather | solution.py:67
  448.2 5.2 fusion
  453.4 0.1 slice.49
  453.5 0.2 reshape.129
  453.7 0.1 fusion.24
  453.8 0.2 fusion.26
  454.0 0.3 slice_negate_fusion
  454.4 0.4 maximum_multiply_fusion
  454.7 0.1 mul.123
  454.8 0.4 fusion.33
  455.2 0.2 fusion.9
  455.3 0.3 fusion.8
  455.7 114.6 %all-gather.14.cloned.1.call-done = bf16[512,4096]{0,1:T(8,128)(2,1)} async-done(((bf16[512,64]{0,1:T(8,128)(2,1)}), bf16[512,4096]{0,1:T(8,128)(2,1)}) %all-gather.14.cloned.1.call-update) | async-done | bytes 4194320 | tf_op jit(solution)/shard_map/all_gather | solution.py:107
  570.2 0.0 copy-start
  570.2 4.9 convolution_convert_fusion
  575.1 0.0 reduce-scatter.2.cloned.1.call-update
  575.1 0.7 pad_maximum_fusion.2
  575.8 87.3 %reduce-scatter.2.cloned.1.call-done = bf16[32,4096]{1,0:T(8,128)(2,1)} async-done(((bf16[256,4096]{1,0:T(8,128)(2,1)}), bf16[32,4096]{1,0:T(8,128)(2,1)}) %reduce-scatter.2.cloned.1.call-update) | async-done | bytes 262160 | tf_op jit(solution)/shard_map/reduce_scatter | solution.py:108
  663.1 0.0 copy-done
  663.1 1.7 fusion.14
  (5 shorter events, 0.1 us)
Async XLA Ops:
  7.2 128.5 %all-gather.10.cloned.1.call-start = ((), (), s32[]{:S(2)}) async-start(), calls=%async_computation.3 | async-start | bytes 1064960 | tf_op jit(solution)/shard_map/all_gather | solution.py:68
  7.9 247.6 %all-gather.12.cloned.1.call-start = ((), (), s32[]{:S(2)}) async-start(), calls=%async_computation.4 | async-start | bytes 1064960 | tf_op jit(solution)/shard_map/all_gather | solution.py:69
  8.6 315.9 %all-gather.6.cloned.1.call-start = ((), (), s32[]{:S(2)}) async-start(), calls=%async_computation.1 | async-start | bytes 2359296 | tf_op jit(solution)/shard_map/all_gather | solution.py:64
  12.3 435.9 %all-gather.8.cloned.1.call-start = ((), (), s32[]{:S(2)}) async-start(), calls=%async_computation.2 | async-start | bytes 4259840 | tf_op jit(solution)/shard_map/all_gather | solution.py:67
  12.9 557.3 %all-gather.14.cloned.1.call-start = ((), (), s32[]{:S(2)}) async-start(), calls=%async_computation.5 | async-start | bytes 4259840 | tf_op jit(solution)/shard_map/all_gather | solution.py:107
  13.5 649.6 %reduce-scatter.2.cloned.1.call-start = ((), (), s32[]{:S(2)}) async-start(), calls=%async_computation.6 | async-start | bytes 2359296 | tf_op jit(solution)/shard_map/reduce_scatter | solution.py:108
  570.2 92.9 %copy-start = (bf16[32,4096]{1,0:T(8,128)(2,1)S(1)}, bf16[32,4096]{1,0:T(8,128)(2,1)}, u32[]{:S(2)}) copy-start(bf16[32,4096]{1,0:T(8,128)(2,1)} %param.7) | copy-start | bytes 786436
Sparse Core Ops, SparseCore 0:
  10.1 125.4 all-gather.9
  137.8 117.6 all-gather.11
  259.3 65.1 all-gather.5
  326.5 121.6 all-gather.7
  450.2 119.9 all-gather.13
  575.2 87.8 reduce-scatter.1
where the time goes:
time: 672 us
  waiting for transfers between devices  635 us (94%)
  between operations  14.2 us (2%)
  matrix products  10.8 us (2%)
  other arithmetic  10.6 us (2%)
    all_gather x1, waiting for transfers between devices, body(): lax.all_gather(w_query, 'dp', axis=0, tiled=True)  124 us
    all_gather x1, waiting for transfers between devices, body(): lax.all_gather(w_value, 'dp', axis=0, tiled=True)  120 us
    all_gather x1, waiting for transfers between devices, body(): lax.all_gather(w_key, 'dp', axis=0, tiled=True)  118 us
    all_gather x1, waiting for transfers between devices, body(): out_full = lax.all_gather(w_out, 'dp', axis=1, tiled=True)  115 us
    reduce_scatter x1, waiting for transfers between devices, body(): lax.psum_scatter(jnp.dot(attended, out_full, preferred_element_type=jnp.f...  87.3 us
    all_gather x1, waiting for transfers between devices, body(): gathered = lax.all_gather(normed, 'tensor', axis=0, tiled=True)  69 us
  transfers between devices with their start and end apart: 6, of which 6 were waited for; matrix products, arithmetic and copies ran while one was open for 2% of the time, Pallas kernels for 0%

commit v1 on v0

--- a/solution.py
+++ b/solution.py
@@ -104,7 +104,8 @@
     attended = (
         jnp.transpose(mixed_rows, (2, 0, 1, 3)).astype(jnp.bfloat16).reshape(pack_rows, query_cols)
     )
-    out_full = lax.all_gather(w_out, "dp", axis=1, tiled=True)
+    sent = jnp.stack([w_out] * lax.axis_size("dp"))
+    out_full = jnp.concatenate(lax.all_to_all(sent, "dp", 0, 0), axis=1)
     summed = lax.psum_scatter(
         jnp.dot(attended, out_full, preferred_element_type=jnp.float32).astype(jnp.bfloat16),
         "tensor",

time: 672 us -> 614 us (0.914)
  waiting for transfers between devices: 635 us -> 562 us
  starting transfers between devices: 0.23 us -> 17.2 us
    all_gather x1 -> x0, waiting for transfers between devices: 115 us -> none  [body(): out_full = lax.all_gather(w_out, 'dp', axis=1, tiled=True)]
    all_gather x1, waiting for transfers between devices: 118 us -> 156 us  [body(): lax.all_gather(w_key, 'dp', axis=0, tiled=True)]
    all_to_all x0 -> x1, starting transfers between devices: none -> 17 us  [body(): out_full = jnp.concatenate(lax.all_to_all(sent, 'dp', 0, 0), axis=1)]
  transfers between devices with their start and end apart: 6 -> 6, of which waited for: 6 -> 5; matrix products, arithmetic and copies ran while one was open for 2% -> 2% of each run, Pallas kernels for 0% -> 0%
where the time goes in v1:
time: 614 us; the launch traced here: 613 us
  waiting for transfers between devices  562 us (92%)
  starting transfers between devices  17.2 us (3%)
  between operations  13.9 us (2%)
  matrix products  10.8 us (2%)
    all_gather x1, waiting for transfers between devices, body(): lax.all_gather(w_key, 'dp', axis=0, tiled=True)  156 us
    all_gather x1, waiting for transfers between devices, body(): lax.all_gather(w_query, 'dp', axis=0, tiled=True)  124 us
    all_gather x1, waiting for transfers between devices, body(): lax.all_gather(w_value, 'dp', axis=0, tiled=True)  123 us
    reduce_scatter x1, waiting for transfers between devices, body(): lax.psum_scatter(jnp.dot(attended, out_full, preferred_element_type=jnp.f...  87.3 us
    all_gather x1, waiting for transfers between devices, body(): gathered = lax.all_gather(normed, 'tensor', axis=0, tiled=True)  70 us
    all_to_all x1, starting transfers between devices, body(): out_full = jnp.concatenate(lax.all_to_all(sent, 'dp', 0, 0), axis=1)  17 us
  transfers between devices with their start and end apart: 6, of which 5 were waited for; matrix products, arithmetic and copies ran while one was open for 2% of the time, Pallas kernels for 0%

profile of v1, /device:TPU:32, one launch (start us, length us, event | category | flops | bytes accessed | tf_op | source)
XLA Modules:
  0.0 613.4 jit_solution(9563754218986794006)
XLA Ops:
  7.2 0.0 all-gather.9.cloned.1.call-start
  7.2 0.7 all-gather.9.cloned.1.call-update
  7.9 0.0 all-gather.11.cloned.1.call-start
  7.9 0.7 all-gather.11.cloned.1.call-update
  8.6 3.3 stack.2
  12.0 0.0 copy-start.2
  12.0 0.0 copy-start
  12.0 0.0 copy-start.1
  12.0 17.0 %all-to-all-start = ((bf16[64,512,64]{1,2,0:T(8,128)(2,1)}), bf16[64,512,64]{1,2,0:T(8,128)(2,1)}, u32[]{:S(2)}, u32[]{:S(2)}) async-start(bf16[64,512,64]{1,2,0:T(8,128)(2,1)} %stack.2), calls=%async_computation | async-start | bytes 8388608 | tf_op jit(solution)/shard_map/all_to_all | solution.py:108
  29.0 0.0 all-gather.5.cloned.1.call-start
  29.0 0.0 copy-done.2
  29.0 0.0 copy-done
  29.1 0.2 fusion.11
  29.2 0.8 fusion.13
  30.1 0.0 all-gather.5.cloned.1.call-update
  30.1 0.0 all-gather.7.cloned.1.call-start
  30.2 0.5 all-gather.7.cloned.1.call-update
  30.7 0.0 reduce-scatter.2.cloned.1.call-start
  30.7 0.0 copy-done.1
  30.7 0.1 slice_compare_fusion
  30.8 0.1 fusion.30
  30.9 0.3 reduce-window.9
  31.2 0.1 slice.38
  31.3 0.1 slice_reduce_fusion
  31.5 0.1 fusion.31
  31.5 0.1 fusion.23
  31.7 0.5 multiply_cosine_fusion
  32.2 156.4 %all-gather.9.cloned.1.call-done = bf16[4096,128]{1,0:T(8,128)(2,1)} async-done(((bf16[64,128]{1,0:T(8,128)(2,1)}), bf16[4096,128]{1,0:T(8,128)(2,1)}) %all-gather.9.cloned.1.call-update) | async-done | bytes 1048592 | tf_op jit(solution)/shard_map/all_gather | solution.py:68
  188.6 122.5 %all-gather.11.cloned.1.call-done = bf16[4096,128]{1,0:T(8,128)(2,1)} async-done(((bf16[64,128]{1,0:T(8,128)(2,1)}), bf16[4096,128]{1,0:T(8,128)(2,1)}) %all-gather.11.cloned.1.call-update) | async-done | bytes 1048592 | tf_op jit(solution)/shard_map/all_gather | solution.py:69
  311.1 70.0 %all-gather.5.cloned.1.call-done = bf16[256,4096]{1,0:T(8,128)(2,1)} async-done(((bf16[32,4096]{1,0:T(8,128)(2,1)}), bf16[256,4096]{1,0:T(8,128)(2,1)}) %all-gather.5.cloned.1.call-update) | async-done | bytes 2097168 | tf_op jit(solution)/shard_map/all_gather | solution.py:64
  381.1 123.7 %all-gather.7.cloned.1.call-done = bf16[4096,512]{1,0:T(8,128)(2,1)} async-done(((bf16[64,512]{1,0:T(8,128)(2,1)}), bf16[4096,512]{1,0:T(8,128)(2,1)}) %all-gather.7.cloned.1.call-update) | async-done | bytes 4194320 | tf_op jit(solution)/shard_map/all_gather | solution.py:67
  504.8 5.2 fusion
  510.1 0.1 slice.49
  510.1 0.2 reshape.137
  510.4 0.1 fusion.24
  510.5 0.2 fusion.26
  510.6 0.3 slice_negate_fusion
  511.0 0.4 maximum_multiply_fusion
  511.3 0.1 mul.123
  511.4 0.4 fusion.33
  511.8 0.2 fusion.9
  512.0 0.3 fusion.8
  512.3 0.0 all-to-all-done
  512.3 4.8 convolution_convert_fusion
  517.1 0.0 reduce-scatter.2.cloned.1.call-update
  517.2 0.7 pad_maximum_fusion.2
  517.8 87.3 %reduce-scatter.2.cloned.1.call-done = bf16[32,4096]{1,0:T(8,128)(2,1)} async-done(((bf16[256,4096]{1,0:T(8,128)(2,1)}), bf16[32,4096]{1,0:T(8,128)(2,1)}) %reduce-scatter.2.cloned.1.call-update) | async-done | bytes 262160 | tf_op jit(solution)/shard_map/reduce_scatter | solution.py:109
  605.2 1.7 fusion.14
  (7 shorter events, 0.1 us)
Async XLA Ops:
  7.2 181.4 %all-gather.9.cloned.1.call-start = ((), (), s32[]{:S(2)}) async-start(), calls=%async_computation.4 | async-start | bytes 1064960 | tf_op jit(solution)/shard_map/all_gather | solution.py:68
  7.9 303.2 %all-gather.11.cloned.1.call-start = ((), (), s32[]{:S(2)}) async-start(), calls=%async_computation.5 | async-start | bytes 1064960 | tf_op jit(solution)/shard_map/all_gather | solution.py:69
  12.0 17.1 %copy-start.2 = (bf16[4096]{0:T(1024)(128)(2,1)S(1)}, bf16[4096]{0:T(1024)(128)(2,1)}, u32[]{:S(2)}) copy-start(bf16[4096]{0:T(1024)(128)(2,1)} %param.8) | copy-start | bytes 24580
  12.0 17.1 %copy-start = (bf16[32,4096]{1,0:T(8,128)(2,1)S(1)}, bf16[32,4096]{1,0:T(8,128)(2,1)}, u32[]{:S(2)}) copy-start(bf16[32,4096]{1,0:T(8,128)(2,1)} %param.7) | copy-start | bytes 786436
  12.0 18.8 %copy-start.1 = (s32[256]{0:T(256)S(1)}, s32[256]{0:T(256)}, u32[]{:S(2)}) copy-start(s32[256]{0:T(256)} %param.13) | copy-start | bytes 3076
  12.0 500.3 %all-to-all-start = ((bf16[64,512,64]{1,2,0:T(8,128)(2,1)}), bf16[64,512,64]{1,2,0:T(8,128)(2,1)}, u32[]{:S(2)}, u32[]{:S(2)}) async-start(bf16[64,512,64]{1,2,0:T(8,128)(2,1)} %stack.2), calls=%async_computation | async-start | bytes 8388608 | tf_op jit(solution)/shard_map/all_to_all | solution.py:108
  29.0 352.2 %all-gather.5.cloned.1.call-start = ((), (), s32[]{:S(2)}) async-start(), calls=%async_computation.2 | async-start | bytes 2359296 | tf_op jit(solution)/shard_map/all_gather | solution.py:64
  30.1 474.7 %all-gather.7.cloned.1.call-start = ((), (), s32[]{:S(2)}) async-start(), calls=%async_computation.3 | async-start | bytes 4259840 | tf_op jit(solution)/shard_map/all_gather | solution.py:67
  30.7 574.5 %reduce-scatter.2.cloned.1.call-start = ((), (), s32[]{:S(2)}) async-start(), calls=%async_computation.6 | async-start | bytes 2359296 | tf_op jit(solution)/shard_map/reduce_scatter | solution.py:109
Sparse Core Ops, SparseCore 0:
  10.1 178.4 all-gather.8
  190.7 120.3 all-gather.10
  314.9 66.1 all-gather.4
  383.1 121.6 all-gather.6
  517.3 87.8 reduce-scatter.1
